TPU v7x, 512 devices: a whole 4x4x16 slice. The times are simulated.
512 devices in a mesh: dp: 32 (over y, z_lo, core), ctx: 16 (over x, z_hi).
Axes of the slice: x: 4, y: 4, z: 16 (z_hi: 4, z_lo: 4; z = z_hi * 4 + z_lo), core: 2. Of those that a mesh axis runs over, the one named last changes fastest.
Arguments:
- branch_in: bfloat16 [32, 2048, 2816], P('dp', 'ctx'), may hold values from -6 to 6
- cotangent: bfloat16 [32, 2048, 2816], P('dp', 'ctx'), may hold values from -6 to 6
- weight_a: bfloat16 [256, 2816], P('dp', 'ctx'), may hold values from -0.375 to 0.375
- weight_x: bfloat16 [256, 2816], P('dp', 'ctx'), may hold values from -0.375 to 0.375
- conv_weight: bfloat16 [4, 2816], P(None, 'ctx'), may hold values from -3 to 3
- conv_bias: bfloat16 [2816], P('ctx'), may hold values from -3 to 3
- bias_a: bfloat16 [2816], P('ctx'), may hold values from -4 to 4
- bias_x: bfloat16 [2816], P('ctx'), may hold values from -4 to 4
- rate: bfloat16 [2816], P('ctx'), may hold values from 0 to 0.016, as said below
Outputs:
- grad_input: bfloat16 [32, 2048, 2816], P('dp', 'ctx')
- grad_weight_a: float32 [256, 2816], P('dp', 'ctx')
- grad_rate: float32 [2816], replicated
Inputs may be any that keep to these rules, and one draw needn't show every extreme that they name: `rate`: positive in every channel.
All inputs are finite; a program needn't handle non-finite values.
Results may differ from a plain program's by a relative error of at most 0.006.
Values may be sent and summed in bfloat16 or wider, within the bound.
No kernel may reach another device: no remote copies, remote signals or barrier semaphores. Data moves between devices by JAX's collectives and lax.ppermute only.
A program may use at most 128 MiB of HBM per device.

v0:
```python
import jax
import jax.numpy as jnp
from jax import lax
from jax.sharding import PartitionSpec as P

floor_value = 2.5e-07
exact = lax.Precision.HIGHEST


def passed_along(array, axis, by):
    length = lax.axis_size(axis)
    pairs = [(i, i + by) for i in range(length) if 0 <= i + by < length]
    return lax.ppermute(array, axis, pairs)


def mix_heads(values, weights):
    tokens = values.shape[0]
    head_width = weights.shape[0]
    head_count = weights.shape[1] // head_width
    left = values.reshape(tokens, head_count, head_width)
    right = weights.reshape(head_width, head_count, head_width)
    result = jnp.einsum("thk,khj->thj", left, right, preferred_element_type=jnp.float32)
    return result.reshape(tokens, head_count * head_width)


def back_heads(grads, weights):
    tokens = grads.shape[0]
    head_width = weights.shape[0]
    head_count = weights.shape[1] // head_width
    left = grads.reshape(tokens, head_count, head_width)
    right = weights.reshape(head_width, head_count, head_width)
    result = jnp.einsum("thj,khj->thk", left, right, preferred_element_type=jnp.float32)
    return result.reshape(tokens, head_count * head_width)


def grad_heads(values, grads, head_width):
    tokens = values.shape[0]
    head_count = values.shape[1] // head_width
    left = values.reshape(tokens, head_count, head_width)
    right = grads.reshape(tokens, head_count, head_width)
    result = jnp.einsum("thk,thj->khj", left, right, preferred_element_type=jnp.float32)
    return result.reshape(head_width, head_count * head_width)


def compose(own, received):
    return (own[0] * received[0], own[0] * received[1] + own[1])


def block_prefix(forward_item, backward_item, axis):
    span = lax.axis_size(axis)
    ones = jnp.ones_like(forward_item[0])
    zeros = jnp.zeros_like(forward_item[0])
    fwd_incl, fwd_excl = (forward_item, (ones, zeros))
    bwd_incl, bwd_excl = (backward_item, (ones, zeros))
    shift = 1
    while shift < span:
        got_fwd = passed_along(jnp.stack(fwd_incl), axis, shift)
        got_bwd = passed_along(jnp.stack(bwd_incl), axis, -shift)
        got_fwd = (got_fwd[0], got_fwd[1])
        got_bwd = (got_bwd[0], got_bwd[1])
        fwd_excl = compose(fwd_excl, got_fwd)
        fwd_incl = compose(fwd_incl, got_fwd)
        bwd_excl = compose(bwd_excl, got_bwd)
        bwd_incl = compose(bwd_incl, got_bwd)
        shift *= 2
    return (fwd_excl[1], bwd_excl[1])


def summed_apart(parts, shared, axis):
    count, size = parts.shape
    stacked = jnp.concatenate([parts, jnp.broadcast_to(shared[None], (count, shared.shape[0]))], 1)
    sublanes = 8
    total = stacked.shape[1]
    tile = sublanes * 256
    padded = -(-total // tile) * tile
    stacked = jnp.pad(stacked, ((0, 0), (0, padded - total)))
    stacked = stacked.reshape(count * sublanes, padded // sublanes)
    mine = lax.psum_scatter(stacked, axis, scatter_dimension=0, tiled=True).reshape(-1)
    return (mine[:size], mine[size:total])


def on_device(
    branch_in, cotangent, weight_a, weight_x, conv_weight, conv_bias, bias_a, bias_x, rate
):
    inputs = branch_in[0]
    upstream = cotangent[0].astype(jnp.float32)
    length = inputs.shape[0]
    taps = conv_weight.shape[0]
    rows, cols = weight_a.shape
    dp_size = lax.axis_size("dp")
    ctx_size = lax.axis_size("ctx")
    packed = jnp.concatenate(
        [conv_weight, conv_bias[None], bias_a[None], bias_x[None], rate[None]], 0
    )
    both = lax.all_gather(jnp.concatenate([weight_a, weight_x], 0), "dp", axis=0, tiled=True)
    both = both.reshape(dp_size, 2, rows, cols).transpose(1, 0, 2, 3)
    head_width = dp_size * rows
    joined = jnp.concatenate([both.reshape(2 * head_width, cols), packed], 0)
    joined = lax.all_gather(joined, "ctx", axis=0, tiled=True)
    joined = joined.reshape(ctx_size, -1, cols).transpose(1, 0, 2).reshape(-1, ctx_size * cols)
    full_a = joined[:head_width]
    full_x = joined[head_width : 2 * head_width]
    params = joined[2 * head_width :]
    params = params.astype(jnp.float32)
    taps_f = params[:taps]
    cbias = params[taps]
    abias = params[taps + 1]
    xbias = params[taps + 2]
    rates = params[taps + 3]
    width = params.shape[1]
    tail = passed_along(inputs[length - (taps - 1) :], "ctx", 1)
    padded = jnp.concatenate([tail, inputs], 0).astype(jnp.float32)
    conv = cbias
    for tap in range(taps):
        conv = conv + taps_f[tap] * padded[tap : tap + length]
    conv_b = conv.astype(jnp.bfloat16)
    conv_f = conv_b.astype(jnp.float32)
    recur_gate = jax.nn.sigmoid(mix_heads(conv_b, full_a) + abias)
    input_gate = jax.nn.sigmoid(mix_heads(conv_b, full_x) + xbias)
    log_decay = -8.0 * recur_gate * rates
    decay = jnp.exp(log_decay)
    one_minus = -jnp.expm1(2.0 * log_decay)
    multiplier = jnp.sqrt(jnp.maximum(one_minus, floor_value))
    drive = multiplier * input_gate * conv_f
    row_id = lax.broadcasted_iota(jnp.int32, (length, length), 0)
    col_id = lax.broadcasted_iota(jnp.int32, (length, length), 1)
    lower = (row_id >= col_id).astype(jnp.float32)
    upper = (row_id <= col_id).astype(jnp.float32)
    cum_log = jnp.dot(lower, log_decay, precision=exact)
    grow = jnp.exp(cum_log)
    shrink = jnp.exp(-cum_log)
    local_hidden = grow * jnp.dot(lower, shrink * drive, precision=exact)
    weighted_back = jnp.dot(upper, grow * upstream, precision=exact)
    local_back = shrink * weighted_back
    block_decay = grow[-1]
    state_in, back_in = block_prefix(
        (block_decay, local_hidden[-1]), (block_decay, weighted_back[0]), "ctx"
    )
    hidden = local_hidden + grow * state_in
    previous = jnp.concatenate([state_in[None], hidden[:-1]], 0)
    back = local_back + block_decay * shrink * back_in
    slope = jnp.where(one_minus > floor_value, 0.5 / multiplier, 0.0)
    d_mult = back * input_gate * conv_f
    d_log = back * previous * decay - 2.0 * decay * decay * d_mult * slope
    d_recur = (d_log * (-8.0 * rates) * recur_gate * (1.0 - recur_gate)).astype(jnp.bfloat16)
    d_input = (back * multiplier * conv_f * input_gate * (1.0 - input_gate)).astype(jnp.bfloat16)
    d_conv = (
        back * multiplier * input_gate + back_heads(d_recur, full_a) + back_heads(d_input, full_x)
    )
    following = passed_along(d_conv[: taps - 1], "ctx", -1)
    dpad = jnp.concatenate([d_conv, following], 0)
    grad_in = jnp.zeros((length, width), jnp.float32)
    for tap in range(taps):
        start = taps - 1 - tap
        grad_in = grad_in + taps_f[tap] * dpad[start : start + length]
    local_wgrad = grad_heads(conv_b, d_recur, head_width)
    local_rgrad = jnp.sum(d_log * (-8.0 * recur_gate), axis=0)
    by_channel = local_wgrad.reshape(head_width, ctx_size, cols).transpose(1, 0, 2)
    channel_sum, rgrad = summed_apart(by_channel.reshape(ctx_size, -1), local_rgrad, "ctx")
    by_row = channel_sum.reshape(dp_size, rows * cols)
    row_sum, rgrad = summed_apart(by_row, rgrad, "dp")
    wgrad = row_sum.reshape(rows, cols)
    return (grad_in.astype(jnp.bfloat16)[None], wgrad, rgrad)


def solution(mesh):
    placed = (
        P("dp", "ctx", None),
        P("dp", "ctx", None),
        P("dp", "ctx"),
        P("dp", "ctx"),
        P(None, "ctx"),
        P("ctx"),
        P("ctx"),
        P("ctx"),
        P("ctx"),
    )
    return jax.shard_map(
        on_device,
        mesh=mesh,
        in_specs=placed,
        out_specs=(P("dp", "ctx", None), P("dp", "ctx"), P()),
        check_vma=False,
    )
```

profile of v0, /device:TPU:2, one launch (start us, length us, event | category | flops | bytes accessed | tf_op | source)
XLA Modules:
  0.0 590.4 jit_solution(10837949532559104495)
XLA Ops:
  7.2 0.7 broadcast_in_dim.18
  7.9 0.7 broadcast_in_dim.36
  8.6 0.7 broadcast_in_dim.37
  9.3 0.7 broadcast_in_dim.38
  9.9 0.7 pad_maximum_fusion.11
  10.6 45.6 %all_gather.6 = bf16[512,176]{1,0:T(8,128)(2,1)S(1)} all-gather(bf16[16,176]{1,0:T(8,128)(2,1)S(1)} %pad_maximum_fusion.11), channel_id=1, replica_groups=mesh['dp'=32,'ctx'=16] {'dp'}, dimensions={0}, use_global_device_ids=true | all-gather | bytes 185856 | tf_op jit(solution)/shard_map/all_gather | solution.py:95
  56.3 0.8 concatenate.22
  57.1 0.8 copy.45
  58.0 9.1 %collective-permute-start = (bf16[3,2816]{1,0:T(4,128)(2,1)S(1)}, bf16[3,2816]{1,0:T(4,128)(2,1)S(1)}, u32[]{:S(2)}, u32[]{:S(2)}) collective-permute-start(bf16[3,2816]{1,0:T(4,128)(2,1)S(1)} %slice_bitcast_fusion), channel_id=1, source_target_pairs={{0,1},{1,2},{2,3},{3,4},{4,5},{5,6},{6,7},{7,8},{8,9},{9,10},{10,1... | collective-permute-start | bytes 50696 | tf_op jit(solution)/shard_map/ppermute | solution.py:13
  67.1 2.8 collective-permute-done
  70.0 0.2 maximum_convert_fusion
  70.1 109.5 %all-gather.3.cloned.1.call-done = bf16[16,520,176]{1,2,0:T(8,128)(2,1)} async-done(((bf16[1,520,176]{1,2,0:T(8,128)(2,1)}), bf16[16,520,176]{1,2,0:T(8,128)(2,1)}) %all-gather.3.cloned.1.call-update) | async-done | bytes 2928656 | tf_op jit(solution)/shard_map/all_gather | solution.py:99
  179.7 1.2 slice_convert_fusion
  180.9 3.1 fusion.45
  184.0 7.0 %slice_reduce_fusion = (f32[16,176]{1,0:T(8,128)S(1)}, f32[16,176]{1,0:T(8,128)S(1)}, f32[16,176]{1,0:T(8,128)S(1)}, f32[16,176]{1,0:T(8,128)S(1)}, f32[16,176]{...) fusion(f32[8,16,176]{0,2,1:T(8,128)S(1)} %slice_convert_fusion), kind=kLoop, calls=%fused_computation.29 | loop fusion | flops 2816 | bytes 180224 | tf_op jit(solution)/shard_map/slice | solution.py:108
  191.7 1.5 fusion.19
  193.2 2.3 copy.46
  195.5 2.8 fusion.48
  198.3 2.9 copy.50
  201.2 3.2 fusion.47
  204.4 2.9 copy.48
  207.3 2.8 fusion.46
  210.2 2.9 convolution_multiply_fusion
  213.2 1.1 fusion.24
  214.4 5.1 collective-permute-start.5
  219.5 5.5 collective-permute-start.1
  225.1 4.1 collective-permute-done.1
  229.2 7.3 %collective-permute-start.6 = (f32[2,2816]{1,0:T(2,128)S(1)}, f32[2,2816]{1,0:T(2,128)S(1)}, u32[]{:S(2)}, u32[]{:S(2)}) collective-permute-start(f32[2,2816]{1,0:T(2,128)S(1)} %pad_maximum_fusion.8), channel_id=1, source_target_pairs={{0,2},{1,3},{2,4},{3,5},{4,6},{5,7},{6,8},{7,9},{8,10},{9,11},{10,... | collective-permute-start | bytes 67592 | tf_op jit(solution)/shard_map/ppermute | solution.py:13
  236.6 8.2 %collective-permute-start.2 = (f32[2,2816]{1,0:T(2,128)S(1)}, f32[2,2816]{1,0:T(2,128)S(1)}, u32[]{:S(2)}, u32[]{:S(2)}) collective-permute-start(f32[2,2816]{1,0:T(2,128)S(1)} %pad_maximum_fusion.5), channel_id=1, source_target_pairs={{2,0},{3,1},{4,2},{5,3},{6,4},{7,5},{8,6},{9,7},{10,8},{11,9},{12,... | collective-permute-start | bytes 67592 | tf_op jit(solution)/shard_map/ppermute | solution.py:13
  244.8 3.4 collective-permute-start.7
  248.2 3.0 collective-permute-done.2
  251.3 2.7 collective-permute-start.3
  254.1 3.8 collective-permute-start.8
  258.0 1.3 collective-permute-start.4
  259.5 0.1 slice_add_fusion
  259.6 5.6 collective-permute-done.4
  265.3 4.6 multiply_reduce_fusion
  269.9 1.3 multiply_convert_fusion
  271.2 1.5 copy.51
  272.7 2.1 fusion.51
  274.9 4.8 copy.60
  279.7 5.8 reshape.115
  285.5 2.1 pad_maximum_fusion
  287.6 1.9 pad.8
  289.5 3.4 reshape.116
  292.9 0.3 reduce-scatter.5.cloned.1.call-start
  293.2 1.1 copy-done
  294.2 2.8 fusion.49
  297.1 3.0 copy.54
  300.1 1.1 copy.55
  301.2 1.7 fusion.50
  302.9 1.5 copy.58
  304.5 127.1 %reduce-scatter.3.cloned.1.call-done = f32[8,6144]{1,0:T(8,128)} async-done(((f32[128,6144]{1,0:T(8,128)}), f32[8,6144]{1,0:T(8,128)}) %reduce-scatter.3.cloned.1.call-update) | async-done | bytes 196624 | tf_op jit(solution)/shard_map/reduce_scatter | solution.py:78
  431.6 1.0 copy.68
  432.7 0.9 pad.9
  433.6 2.3 reshape.119
  435.9 2.2 add_add_fusion
  438.2 5.8 collective-permute-start.9
  444.0 4.0 collective-permute-done.9
  448.0 1.5 fusion.34
  449.5 132.4 %reduce-scatter.5.cloned.1.call-done = f32[8,768]{1,0:T(8,128)} async-done(((f32[256,768]{1,0:T(8,128)}), f32[8,768]{1,0:T(8,128)}) %reduce-scatter.5.cloned.1.call-update) | async-done | bytes 24592 | tf_op jit(solution)/shard_map/reduce_scatter | solution.py:78
  581.9 0.7 reshape.120
  582.6 0.6 slice.234
  583.2 0.7 reshape.121
  (66 shorter events, 1.7 us)
Async XLA Ops:
  7.2 50.8 %copy-start.9 = (bf16[1,128,2816]{2,1,0:T(8,128)(2,1)S(1)}, bf16[1,128,2816]{2,1,0:T(8,128)(2,1)}, u32[]{:S(2)}) copy-start(bf16[1,128,2816]{2,1,0:T(8,128)(2,1)} %param.9) | copy-start | bytes 2162692
  7.2 172.5 %all-gather.3.cloned.1.call-start = ((), (), s32[]{:S(2)}) async-start(), calls=%async_computation.4 | async-start | bytes 3829760 | tf_op jit(solution)/shard_map/all_gather | solution.py:99
  57.9 373.6 %reduce-scatter.3.cloned.1.call-start = ((), (), s32[]{:S(2)}) async-start(), calls=%async_computation.2 | async-start | bytes 3342336 | tf_op jit(solution)/shard_map/reduce_scatter | solution.py:78
  58.0 11.9 %collective-permute-start = (bf16[3,2816]{1,0:T(4,128)(2,1)S(1)}, bf16[3,2816]{1,0:T(4,128)(2,1)S(1)}, u32[]{:S(2)}, u32[]{:S(2)}) collective-permute-start(bf16[3,2816]{1,0:T(4,128)(2,1)S(1)} %slice_bitcast_fusion), channel_id=1, source_target_pairs={{0,1},{1,2},{2,3},{3,4},{4,5},{5,6},{6,7},{7,8},{8,9},{9,10},{10,1... | collective-permute-start | bytes 50696 | tf_op jit(solution)/shard_map/ppermute | solution.py:13
  207.3 2.8 copy-start.1
  207.3 2.9 copy-start.2
  207.3 2.9 copy-start.8
  210.2 3.0 copy-start.10
  214.4 10.7 %collective-permute-start.5 = (f32[2,2816]{1,0:T(2,128)S(1)}, f32[2,2816]{1,0:T(2,128)S(1)}, u32[]{:S(2)}, u32[]{:S(2)}) collective-permute-start(f32[2,2816]{1,0:T(2,128)S(1)} %get-tuple-element.36), channel_id=1, source_target_pairs={{0,1},{1,2},{2,3},{3,4},{4,5},{5,6},{6,7},{7,8},{8,9},{9,10},{10,1... | collective-permute-start | bytes 67592 | tf_op jit(solution)/shard_map/ppermute | solution.py:13
  219.5 9.6 %collective-permute-start.1 = (f32[2,2816]{1,0:T(2,128)S(1)}, f32[2,2816]{1,0:T(2,128)S(1)}, u32[]{:S(2)}, u32[]{:S(2)}) collective-permute-start(f32[2,2816]{1,0:T(2,128)S(1)} %get-tuple-element.37), channel_id=1, source_target_pairs={{1,0},{2,1},{3,2},{4,3},{5,4},{6,5},{7,6},{8,7},{9,8},{10,9},{11,1... | collective-permute-start | bytes 67592 | tf_op jit(solution)/shard_map/ppermute | solution.py:13
  229.2 15.5 %collective-permute-start.6 = (f32[2,2816]{1,0:T(2,128)S(1)}, f32[2,2816]{1,0:T(2,128)S(1)}, u32[]{:S(2)}, u32[]{:S(2)}) collective-permute-start(f32[2,2816]{1,0:T(2,128)S(1)} %pad_maximum_fusion.8), channel_id=1, source_target_pairs={{0,2},{1,3},{2,4},{3,5},{4,6},{5,7},{6,8},{7,9},{8,10},{9,11},{10,... | collective-permute-start | bytes 67592 | tf_op jit(solution)/shard_map/ppermute | solution.py:13
  236.6 14.6 %collective-permute-start.2 = (f32[2,2816]{1,0:T(2,128)S(1)}, f32[2,2816]{1,0:T(2,128)S(1)}, u32[]{:S(2)}, u32[]{:S(2)}) collective-permute-start(f32[2,2816]{1,0:T(2,128)S(1)} %pad_maximum_fusion.5), channel_id=1, source_target_pairs={{2,0},{3,1},{4,2},{5,3},{6,4},{7,5},{8,6},{9,7},{10,8},{11,9},{12,... | collective-permute-start | bytes 67592 | tf_op jit(solution)/shard_map/ppermute | solution.py:13
  244.8 9.2 %collective-permute-start.7 = (f32[2,2816]{1,0:T(2,128)S(1)}, f32[2,2816]{1,0:T(2,128)S(1)}, u32[]{:S(2)}, u32[]{:S(2)}) collective-permute-start(f32[2,2816]{1,0:T(2,128)S(1)} %pad_maximum_fusion.9), channel_id=1, source_target_pairs={{0,4},{1,5},{2,6},{3,7},{4,8},{5,9},{6,10},{7,11},{8,12},{9,13},{1... | collective-permute-start | bytes 67592 | tf_op jit(solution)/shard_map/ppermute | solution.py:13
  251.3 6.7 %collective-permute-start.3 = (f32[2,2816]{1,0:T(2,128)S(1)}, f32[2,2816]{1,0:T(2,128)S(1)}, u32[]{:S(2)}, u32[]{:S(2)}) collective-permute-start(f32[2,2816]{1,0:T(2,128)S(1)} %pad_maximum_fusion.6), channel_id=1, source_target_pairs={{4,0},{5,1},{6,2},{7,3},{8,4},{9,5},{10,6},{11,7},{12,8},{13,9},{1... | collective-permute-start | bytes 67592 | tf_op jit(solution)/shard_map/ppermute | solution.py:13
  254.1 5.3 collective-permute-start.8
  258.0 7.2 %collective-permute-start.4 = (f32[2,2816]{1,0:T(2,128)S(1)}, f32[2,2816]{1,0:T(2,128)S(1)}, u32[]{:S(2)}, u32[]{:S(2)}) collective-permute-start(f32[2,2816]{1,0:T(2,128)S(1)} %pad_maximum_fusion.7), channel_id=1, source_target_pairs={{8,0},{9,1},{10,2},{11,3},{12,4},{13,5},{14,6},{15,7},{24,16},{25,... | collective-permute-start | bytes 67592 | tf_op jit(solution)/shard_map/ppermute | solution.py:13
  271.2 1.5 copy-start.4
  272.7 2.2 copy-start.5
  292.9 1.4 copy-start
  292.9 289.0 %reduce-scatter.5.cloned.1.call-start = ((), (), s32[]{:S(2)}) async-start(), calls=%async_computation.3 | async-start | bytes 811008 | tf_op jit(solution)/shard_map/reduce_scatter | solution.py:78
  297.1 3.0 copy-start.7
  432.7 3.2 copy-start.6
  433.6 2.3 copy-start.3
  438.2 9.8 %collective-permute-start.9 = (f32[3,2816]{1,0:T(4,128)S(1)}, f32[3,2816]{1,0:T(4,128)S(1)}, u32[]{:S(2)}, u32[]{:S(2)}) collective-permute-start(f32[3,2816]{1,0:T(4,128)S(1)} %slice.226), channel_id=1, source_target_pairs={{1,0},{2,1},{3,2},{4,3},{5,4},{6,5},{7,6},{8,7},{9,8},{10,9},{11,1... | collective-permute-start | bytes 101384 | tf_op jit(solution)/shard_map/ppermute | solution.py:13
Sparse Core Ops, SparseCore 0:
  58.1 121.5 all-gather.2
  293.0 138.5 reduce-scatter.2
  436.0 145.7 reduce-scatter.4
where the time goes:
time: 592 us; the launch traced here: 590 us
  waiting for transfers between devices  389 us (66%)
  starting transfers between devices  52.6 us (9%)
  local copies, waits for them, and re-layouts  46.7 us (8%)
  blocking collectives  45.6 us (8%)
  other arithmetic  23.1 us (4%)
  matrix products  19.6 us (3%)
  between operations  14.2 us (2%)
    reduce_scatter x2, waiting for transfers between devices, summed_apart(): lax.psum_scatter(stacked, axis, scatter_dimension=0, tiled=True).reshape(-1)  259 us
    all_gather x1, waiting for transfers between devices, on_device(): joined = lax.all_gather(joined, 'ctx', axis=0, tiled=True)  110 us
    ppermute x10, starting transfers between devices, passed_along(): return lax.ppermute(array, axis, pairs)  52.2 us
    all_gather x1, blocking collectives, on_device(): lax.all_gather(jnp.concatenate([weight_a, weight_x], 0), 'dp', axis=0, ti...  45.6 us
    ppermute x10, waiting for transfers between devices, passed_along(): return lax.ppermute(array, axis, pairs)  19.6 us
  transfers between devices with their start and end apart: 13, of which 9 were waited for; matrix products, arithmetic and copies ran while one was open for 2% of the time, Pallas kernels for 0%

commit v1 on v0

--- a/solution.py
+++ b/solution.py
@@ -96,7 +96,9 @@
     both = both.reshape(dp_size, 2, rows, cols).transpose(1, 0, 2, 3)
     head_width = dp_size * rows
     joined = jnp.concatenate([both.reshape(2 * head_width, cols), packed], 0)
-    joined = lax.all_gather(joined, "ctx", axis=0, tiled=True)
+    joined = jnp.concatenate(
+        lax.all_to_all(jnp.stack([joined] * lax.axis_size("ctx")), "ctx", 0, 0), axis=0
+    )
     joined = joined.reshape(ctx_size, -1, cols).transpose(1, 0, 2).reshape(-1, ctx_size * cols)
     full_a = joined[:head_width]
     full_x = joined[head_width : 2 * head_width]

time: 592 us -> 665 us (1.12)
  waiting for transfers between devices: 389 us -> 439 us
  starting transfers between devices: 52.6 us -> 73.9 us
    ppermute x10, waiting for transfers between devices: 19.6 us -> 173 us  [passed_along(): return lax.ppermute(array, axis, pairs)]
    all_gather x1 -> x0, waiting for transfers between devices: 110 us -> none  [on_device(): joined = lax.all_gather(joined, 'ctx', axis=0, tiled=True)]
    all_to_all x0 -> x1, starting transfers between devices: none -> 15.5 us  [on_device(): lax.all_to_all(jnp.stack([joined] * lax.axis_size('ctx')), 'ctx', 0, 0)]
where the time goes in v1:
time: 665 us; the launch traced here: 664 us
  waiting for transfers between devices  439 us (66%)
  starting transfers between devices  73.9 us (11%)
  local copies, waits for them, and re-layouts  48.1 us (7%)
  blocking collectives  45.6 us (7%)
  other arithmetic  23.1 us (3%)
  matrix products  19.6 us (3%)
  between operations  14.5 us (2%)
    reduce_scatter x2, waiting for transfers between devices, summed_apart(): lax.psum_scatter(stacked, axis, scatter_dimension=0, tiled=True).reshape(-1)  263 us
    ppermute x10, waiting for transfers between devices, passed_along(): return lax.ppermute(array, axis, pairs)  173 us
    ppermute x10, starting transfers between devices, passed_along(): return lax.ppermute(array, axis, pairs)  58.1 us
    all_gather x1, blocking collectives, on_device(): lax.all_gather(jnp.concatenate([weight_a, weight_x], 0), 'dp', axis=0, ti...  45.6 us
    all_to_all x1, starting transfers between devices, on_device(): lax.all_to_all(jnp.stack([joined] * lax.axis_size('ctx')), 'ctx', 0, 0)  15.5 us
  transfers between devices with their start and end apart: 13, of which 9 were waited for; matrix products, arithmetic and copies ran while one was open for 2% of the time, Pallas kernels for 0%

profile of v1, /device:TPU:2, one launch (start us, length us, event | category | flops | bytes accessed | tf_op | source)
XLA Modules:
  0.0 664.2 jit_solution(6726143454927356619)
XLA Ops:
  7.2 0.7 broadcast_in_dim.18
  7.8 0.7 broadcast_in_dim.36
  8.5 0.7 broadcast_in_dim.37
  9.1 0.7 broadcast_in_dim.38
  9.8 0.7 pad_maximum_fusion.11
  10.5 45.6 %all_gather.3 = bf16[512,176]{1,0:T(8,128)(2,1)S(1)} all-gather(bf16[16,176]{1,0:T(8,128)(2,1)S(1)} %pad_maximum_fusion.11), channel_id=1, replica_groups=mesh['dp'=32,'ctx'=16] {'dp'}, dimensions={0}, use_global_device_ids=true | all-gather | bytes 185856 | tf_op jit(solution)/shard_map/all_gather | solution.py:95
  56.2 0.8 concatenate.22
  57.1 2.1 stack.18
  59.3 15.5 %all-to-all-start = ((bf16[16,520,176]{1,2,0:T(8,128)(2,1)}), bf16[16,520,176]{1,2,0:T(8,128)(2,1)}, u32[]{:S(2)}, u32[]{:S(2)}) async-start(bf16[16,520,176]{1,2,0:T(8,128)(2,1)} %stack.18), calls=%async_computation | async-start | bytes 7208960 | tf_op jit(solution)/shard_map/all_to_all | solution.py:100
  74.9 7.3 %collective-permute-start = (bf16[3,2816]{1,0:T(4,128)(2,1)S(1)}, bf16[3,2816]{1,0:T(4,128)(2,1)S(1)}, u32[]{:S(2)}, u32[]{:S(2)}) collective-permute-start(bf16[3,2816]{1,0:T(4,128)(2,1)S(1)} %slice_bitcast_fusion), channel_id=1, source_target_pairs={{0,1},{1,2},{2,3},{3,4},{4,5},{5,6},{6,7},{7,8},{8,9},{9,10},{10,1... | collective-permute-start | bytes 50696 | tf_op jit(solution)/shard_map/ppermute | solution.py:13
  82.1 150.9 %collective-permute-done = bf16[3,2816]{1,0:T(4,128)(2,1)S(1)} collective-permute-done((bf16[3,2816]{1,0:T(4,128)(2,1)S(1)}, bf16[3,2816]{1,0:T(4,128)(2,1)S(1)}, u32[]{:S(2)}, u32[]{:S(2)}) %collective-permute-start) | collective-permute-done | bytes 16928 | tf_op jit(solution)/shard_map/ppermute | solution.py:13
  233.2 3.4 all-to-all-done
  236.6 1.2 slice_convert_fusion
  237.8 3.1 fusion.45
  240.9 7.0 %slice_reduce_fusion = (f32[16,176]{1,0:T(8,128)S(1)}, f32[16,176]{1,0:T(8,128)S(1)}, f32[16,176]{1,0:T(8,128)S(1)}, f32[16,176]{1,0:T(8,128)S(1)}, f32[16,176]{...) fusion(f32[8,16,176]{0,2,1:T(8,128)S(1)} %slice_convert_fusion), kind=kLoop, calls=%fused_computation.29 | loop fusion | flops 2816 | bytes 180224 | tf_op jit(solution)/shard_map/slice | solution.py:110
  248.6 1.5 fusion.19
  250.1 2.3 copy.45
  252.4 2.8 fusion.48
  255.2 2.9 copy.49
  258.1 3.2 fusion.47
  261.4 2.9 copy.47
  264.3 2.8 fusion.46
  267.2 2.9 convolution_multiply_fusion
  270.1 1.1 fusion.24
  271.3 4.9 collective-permute-start.5
  276.2 16.6 %collective-permute-start.1 = (f32[2,2816]{1,0:T(2,128)S(1)}, f32[2,2816]{1,0:T(2,128)S(1)}, u32[]{:S(2)}, u32[]{:S(2)}) collective-permute-start(f32[2,2816]{1,0:T(2,128)S(1)} %get-tuple-element.37), channel_id=1, source_target_pairs={{1,0},{2,1},{3,2},{4,3},{5,4},{6,5},{7,6},{8,7},{9,8},{10,9},{11,1... | collective-permute-start | bytes 67592 | tf_op jit(solution)/shard_map/ppermute | solution.py:13
  292.8 7.3 %collective-permute-done.1 = f32[2,2816]{1,0:T(2,128)S(1)} collective-permute-done((f32[2,2816]{1,0:T(2,128)S(1)}, f32[2,2816]{1,0:T(2,128)S(1)}, u32[]{:S(2)}, u32[]{:S(2)}) %collective-permute-start.1) | collective-permute-done | bytes 22560 | tf_op jit(solution)/shard_map/ppermute | solution.py:13
  300.2 7.3 %collective-permute-start.6 = (f32[2,2816]{1,0:T(2,128)S(1)}, f32[2,2816]{1,0:T(2,128)S(1)}, u32[]{:S(2)}, u32[]{:S(2)}) collective-permute-start(f32[2,2816]{1,0:T(2,128)S(1)} %pad_maximum_fusion.8), channel_id=1, source_target_pairs={{0,2},{1,3},{2,4},{3,5},{4,6},{5,7},{6,8},{7,9},{8,10},{9,11},{10,... | collective-permute-start | bytes 67592 | tf_op jit(solution)/shard_map/ppermute | solution.py:13
  307.5 8.2 %collective-permute-start.2 = (f32[2,2816]{1,0:T(2,128)S(1)}, f32[2,2816]{1,0:T(2,128)S(1)}, u32[]{:S(2)}, u32[]{:S(2)}) collective-permute-start(f32[2,2816]{1,0:T(2,128)S(1)} %pad_maximum_fusion.5), channel_id=1, source_target_pairs={{2,0},{3,1},{4,2},{5,3},{6,4},{7,5},{8,6},{9,7},{10,8},{11,9},{12,... | collective-permute-start | bytes 67592 | tf_op jit(solution)/shard_map/ppermute | solution.py:13
  315.8 1.9 collective-permute-start.7
  317.7 4.2 collective-permute-done.2
  322.0 3.6 collective-permute-start.3
  325.7 1.3 collective-permute-start.8
  327.0 0.7 collective-permute-done.3
  327.8 1.3 collective-permute-start.4
  329.3 5.7 collective-permute-done.4
  335.0 4.6 multiply_reduce_fusion
  339.7 1.3 multiply_convert_fusion
  341.0 1.5 copy.50
  342.5 2.1 fusion.51
  344.7 4.8 copy.59
  349.5 5.8 reshape.113
  355.3 2.1 pad_maximum_fusion
  357.4 1.9 pad.8
  359.3 3.4 reshape.114
  362.7 0.3 reduce-scatter.5.cloned.1.call-start
  363.0 1.1 copy-done
  364.0 2.8 fusion.49
  366.8 3.0 copy.53
  369.9 1.1 copy.54
  371.0 1.7 fusion.50
  372.7 1.5 copy.57
  374.2 130.9 %reduce-scatter.3.cloned.1.call-done = f32[8,6144]{1,0:T(8,128)} async-done(((f32[128,6144]{1,0:T(8,128)}), f32[8,6144]{1,0:T(8,128)}) %reduce-scatter.3.cloned.1.call-update) | async-done | bytes 196624 | tf_op jit(solution)/shard_map/reduce_scatter | solution.py:78
  505.1 1.0 copy.67
  506.2 0.9 pad.9
  507.2 2.3 reshape.117
  509.5 2.2 add_add_fusion
  511.7 5.8 collective-permute-start.9
  517.5 4.0 collective-permute-done.9
  521.5 1.5 fusion.34
  523.0 132.3 %reduce-scatter.5.cloned.1.call-done = f32[8,768]{1,0:T(8,128)} async-done(((f32[256,768]{1,0:T(8,128)}), f32[8,768]{1,0:T(8,128)}) %reduce-scatter.5.cloned.1.call-update) | async-done | bytes 24592 | tf_op jit(solution)/shard_map/reduce_scatter | solution.py:78
  655.3 0.7 reshape.118
  656.1 0.6 slice.234
  656.7 0.7 reshape.119
  (66 shorter events, 2.0 us)
Async XLA Ops:
  59.2 15.6 %copy-start.9 = (bf16[1,128,2816]{2,1,0:T(8,128)(2,1)S(1)}, bf16[1,128,2816]{2,1,0:T(8,128)(2,1)}, u32[]{:S(2)}) copy-start(bf16[1,128,2816]{2,1,0:T(8,128)(2,1)} %param.9) | copy-start | bytes 2162692
  59.3 177.3 %all-to-all-start = ((bf16[16,520,176]{1,2,0:T(8,128)(2,1)}), bf16[16,520,176]{1,2,0:T(8,128)(2,1)}, u32[]{:S(2)}, u32[]{:S(2)}) async-start(bf16[16,520,176]{1,2,0:T(8,128)(2,1)} %stack.18), calls=%async_computation | async-start | bytes 7208960 | tf_op jit(solution)/shard_map/all_to_all | solution.py:100
  74.8 430.3 %reduce-scatter.3.cloned.1.call-start = ((), (), s32[]{:S(2)}) async-start(), calls=%async_computation.3 | async-start | bytes 3342336 | tf_op jit(solution)/shard_map/reduce_scatter | solution.py:78
  74.9 158.2 %collective-permute-start = (bf16[3,2816]{1,0:T(4,128)(2,1)S(1)}, bf16[3,2816]{1,0:T(4,128)(2,1)S(1)}, u32[]{:S(2)}, u32[]{:S(2)}) collective-permute-start(bf16[3,2816]{1,0:T(4,128)(2,1)S(1)} %slice_bitcast_fusion), channel_id=1, source_target_pairs={{0,1},{1,2},{2,3},{3,4},{4,5},{5,6},{6,7},{7,8},{8,9},{9,10},{10,1... | collective-permute-start | bytes 50696 | tf_op jit(solution)/shard_map/ppermute | solution.py:13
  264.3 2.8 copy-start.1
  264.3 2.9 copy-start.2
  264.3 2.9 copy-start.8
  267.2 3.0 copy-start.10
  271.3 21.5 %collective-permute-start.5 = (f32[2,2816]{1,0:T(2,128)S(1)}, f32[2,2816]{1,0:T(2,128)S(1)}, u32[]{:S(2)}, u32[]{:S(2)}) collective-permute-start(f32[2,2816]{1,0:T(2,128)S(1)} %get-tuple-element.36), channel_id=1, source_target_pairs={{0,1},{1,2},{2,3},{3,4},{4,5},{5,6},{6,7},{7,8},{8,9},{9,10},{10,1... | collective-permute-start | bytes 67592 | tf_op jit(solution)/shard_map/ppermute | solution.py:13
  276.2 23.9 %collective-permute-start.1 = (f32[2,2816]{1,0:T(2,128)S(1)}, f32[2,2816]{1,0:T(2,128)S(1)}, u32[]{:S(2)}, u32[]{:S(2)}) collective-permute-start(f32[2,2816]{1,0:T(2,128)S(1)} %get-tuple-element.37), channel_id=1, source_target_pairs={{1,0},{2,1},{3,2},{4,3},{5,4},{6,5},{7,6},{8,7},{9,8},{10,9},{11,1... | collective-permute-start | bytes 67592 | tf_op jit(solution)/shard_map/ppermute | solution.py:13
  300.2 15.5 %collective-permute-start.6 = (f32[2,2816]{1,0:T(2,128)S(1)}, f32[2,2816]{1,0:T(2,128)S(1)}, u32[]{:S(2)}, u32[]{:S(2)}) collective-permute-start(f32[2,2816]{1,0:T(2,128)S(1)} %pad_maximum_fusion.8), channel_id=1, source_target_pairs={{0,2},{1,3},{2,4},{3,5},{4,6},{5,7},{6,8},{7,9},{8,10},{9,11},{10,... | collective-permute-start | bytes 67592 | tf_op jit(solution)/shard_map/ppermute | solution.py:13
  307.5 14.4 %collective-permute-start.2 = (f32[2,2816]{1,0:T(2,128)S(1)}, f32[2,2816]{1,0:T(2,128)S(1)}, u32[]{:S(2)}, u32[]{:S(2)}) collective-permute-start(f32[2,2816]{1,0:T(2,128)S(1)} %pad_maximum_fusion.5), channel_id=1, source_target_pairs={{2,0},{3,1},{4,2},{5,3},{6,4},{7,5},{8,6},{9,7},{10,8},{11,9},{12,... | collective-permute-start | bytes 67592 | tf_op jit(solution)/shard_map/ppermute | solution.py:13
  315.8 9.8 %collective-permute-start.7 = (f32[2,2816]{1,0:T(2,128)S(1)}, f32[2,2816]{1,0:T(2,128)S(1)}, u32[]{:S(2)}, u32[]{:S(2)}) collective-permute-start(f32[2,2816]{1,0:T(2,128)S(1)} %pad_maximum_fusion.9), channel_id=1, source_target_pairs={{0,4},{1,5},{2,6},{3,7},{4,8},{5,9},{6,10},{7,11},{8,12},{9,13},{1... | collective-permute-start | bytes 67592 | tf_op jit(solution)/shard_map/ppermute | solution.py:13
  322.0 5.7 collective-permute-start.3
  325.7 3.4 collective-permute-start.8
  327.8 7.2 %collective-permute-start.4 = (f32[2,2816]{1,0:T(2,128)S(1)}, f32[2,2816]{1,0:T(2,128)S(1)}, u32[]{:S(2)}, u32[]{:S(2)}) collective-permute-start(f32[2,2816]{1,0:T(2,128)S(1)} %pad_maximum_fusion.7), channel_id=1, source_target_pairs={{8,0},{9,1},{10,2},{11,3},{12,4},{13,5},{14,6},{15,7},{24,16},{25,... | collective-permute-start | bytes 67592 | tf_op jit(solution)/shard_map/ppermute | solution.py:13
  341.0 1.5 copy-start.4
  342.5 2.2 copy-start.5
  362.7 1.4 copy-start
  362.7 292.6 %reduce-scatter.5.cloned.1.call-start = ((), (), s32[]{:S(2)}) async-start(), calls=%async_computation.4 | async-start | bytes 811008 | tf_op jit(solution)/shard_map/reduce_scatter | solution.py:78
  366.8 3.0 copy-start.7
  506.2 3.2 copy-start.6
  507.2 2.3 copy-start.3
  511.7 9.8 %collective-permute-start.9 = (f32[3,2816]{1,0:T(4,128)S(1)}, f32[3,2816]{1,0:T(4,128)S(1)}, u32[]{:S(2)}, u32[]{:S(2)}) collective-permute-start(f32[3,2816]{1,0:T(4,128)S(1)} %slice.226), channel_id=1, source_target_pairs={{1,0},{2,1},{3,2},{4,3},{5,4},{6,5},{7,6},{8,7},{9,8},{10,9},{11,1... | collective-permute-start | bytes 101384 | tf_op jit(solution)/shard_map/ppermute | solution.py:13
Sparse Core Ops, SparseCore 0:
  362.8 142.2 reduce-scatter.2
  509.6 145.7 reduce-scatter.4
